TPU v7x, 32 devices: a whole 2x2x4 slice. The times are simulated.
32 devices in a mesh: pw: 8 (over z, y), band: 4 (over x, core).
Axes of the slice: x: 2, y: 2, z: 4, core: 2. Of those that a mesh axis runs over, the one named last changes fastest.
Arguments:
- psi_block: float32 [2, 8, 256, 128], P(None, 'band', 'pw'), may hold values from -6 to 6
- psi_all: bfloat16 [2, 1024, 256, 128], P(None, 'band', 'pw'), may hold values from -0.0234375 to 0.0234375
- potential: float32 [128, 128, 128], P('pw'), may hold values from -8 to 8
- stick_col: int32 [256], replicated, may hold values from 0 to 16383, as said below
Outputs:
- intersection: float32 [2, 8, 1024], P(None, 'pw', 'band')
- hpsi: float32 [2, 8, 256, 128], P(None, 'band', 'pw')
Inputs may be any that keep to these rules, and one draw needn't show every extreme that they name: `stick_col`: distinct columns of the 128 x 128 plane; column 0 and column 16383 are always among them.
All inputs are finite; a program needn't handle non-finite values.
Results may differ from a plain program's by a relative error of at most 0.0029.
Values may be sent and summed in bfloat16 or wider, within the bound.
No kernel may reach another device: no remote copies, remote signals or barrier semaphores. Data moves between devices by JAX's collectives and lax.ppermute only.
A program may use at most 64 MiB of HBM per device.

v0:
```python
import math
import jax
import numpy as np
import jax.numpy as jnp
from jax import lax
from jax.sharding import PartitionSpec as P


def frequency(index, size):
    return jnp.where(index < size // 2, index, index - size)


def kinetic_table(columns, grid_size):
    col_x = frequency(columns // grid_size, grid_size).astype(jnp.float32)
    col_y = frequency(columns % grid_size, grid_size).astype(jnp.float32)
    along = frequency(jnp.arange(grid_size, dtype=jnp.int32), grid_size).astype(jnp.float32)
    plane = col_x * col_x + col_y * col_y
    return 4.0 * (plane[:, None] + along[None, :] * along[None, :]) / float(grid_size * grid_size)


def dft_table(grid_size, sign):
    indices = np.arange(grid_size)
    products = indices[:, None] * indices[None, :] % grid_size
    angles = 2.0 * np.pi / grid_size * products
    cosine = np.cos(angles)
    sine = sign * np.sin(angles)
    table = np.stack([np.stack([cosine, -sine]), np.stack([sine, cosine])])
    return jnp.asarray(table.astype(np.float32))


def plane_tables(stick_col, grid_size):
    grid_iota = jnp.arange(grid_size, dtype=jnp.int32)
    col_x = stick_col // grid_size
    col_y = stick_col % grid_size
    phase_angles = (
        2.0
        * math.pi
        / grid_size
        * (grid_iota[:, None] * col_x[None, :] % grid_size).astype(jnp.float32)
    )
    place_cols = (col_y[:, None] == grid_iota[None, :]).astype(jnp.float32)
    pick_cols = (grid_iota[:, None] == col_y[None, :]).astype(jnp.float32)
    return (jnp.cos(phase_angles), jnp.sin(phase_angles), place_cols, pick_cols)


def mult(left, right):
    return jnp.dot(left, right, precision=lax.Precision.HIGH, preferred_element_type=jnp.float32)


def plane_phase(amp, pot, tables, grid_size):
    phase_cos, phase_sin, place_cols, pick_cols = tables
    inverse = dft_table(grid_size, 1.0)
    cosine = inverse[0, 0]
    sine = inverse[1, 0]
    scaled_pot = (pot / float(grid_size**3))[None]
    val_re = amp[0][:, :, None, :]
    val_im = amp[1][:, :, None, :]
    spread_re = val_re * phase_cos - val_im * phase_sin
    spread_im = val_re * phase_sin + val_im * phase_cos
    rows_re = mult(spread_re, place_cols)
    rows_im = mult(spread_im, place_cols)
    shared = mult(rows_re + rows_im, cosine)
    wave_re = (shared - mult(rows_im, cosine + sine)) * scaled_pot
    wave_im = (shared + mult(rows_re, sine - cosine)) * scaled_pot
    shared = mult(wave_re + wave_im, cosine)
    back_re = shared - mult(wave_im, cosine - sine)
    back_im = shared - mult(wave_re, sine + cosine)
    sel_re = mult(back_re, pick_cols)
    sel_im = mult(back_im, pick_cols)
    picked_re = jnp.sum(sel_re * phase_cos + sel_im * phase_sin, axis=2)
    picked_im = jnp.sum(sel_im * phase_cos - sel_re * phase_sin, axis=2)
    return jnp.stack([picked_re, picked_im])


def intersect(lowered, psi_all, pw_count):
    turned = jnp.stack([-lowered[1], lowered[0]])
    both = jnp.concatenate([lowered, turned], axis=1)
    dims = (((2, 3), (2, 3)), ((0,), (0,)))
    width = psi_all.shape[1] // 4
    partial_value = jnp.concatenate(
        [
            jnp.sum(
                lax.dot_general(
                    both,
                    psi_all[:, k * width : (k + 1) * width],
                    dims,
                    preferred_element_type=jnp.float32,
                ),
                axis=0,
            )
            for k in range(4)
        ],
        axis=-1,
    )
    partial_value = partial_value.reshape(2, lowered.shape[1], partial_value.shape[-1])
    rows_dev = partial_value.shape[1] // pw_count
    pieces = partial_value.reshape(2, pw_count, rows_dev, partial_value.shape[-1])
    pieces = lax.all_to_all(pieces, "pw", split_axis=1, concat_axis=1, tiled=True)
    return jnp.sum(pieces, axis=1)


def per_device_rows(psi_block, psi_all, potential, stick_col):
    sticks_dev = psi_block.shape[2]
    grid_size = psi_block.shape[3]
    fast = lax.Precision.HIGH
    rank = lax.axis_index("pw")
    pw_count = lax.axis_size("pw")
    planes = potential.shape[0]
    my_columns = lax.dynamic_slice_in_dim(stick_col, rank * sticks_dev, sticks_dev)
    kinetic = kinetic_table(my_columns, grid_size)
    inverse = dft_table(grid_size, 1.0)
    forward = dft_table(grid_size, -1.0)
    tables = plane_tables(stick_col, grid_size)
    parts = []
    for band in range(psi_block.shape[1]):
        coeffs = psi_block[:, band : band + 1]
        z_lines = jnp.einsum("dczk,cbsk->zdbs", inverse, coeffs, precision=fast)
        received = lax.all_to_all(z_lines, "pw", split_axis=0, concat_axis=0, tiled=True)
        lanes = received.shape[1:]
        received = received.reshape((pw_count, planes) + lanes)
        amp = jnp.transpose(received, (2, 3, 1, 0, 4)).reshape(
            lanes[0], lanes[1], planes, pw_count * sticks_dev
        )
        picked = plane_phase(amp, potential, tables, grid_size)
        outgoing = picked.reshape(lanes[0], lanes[1], planes, pw_count, sticks_dev)
        outgoing = jnp.transpose(outgoing, (3, 2, 0, 1, 4)).reshape((pw_count * planes,) + lanes)
        sticks_back = lax.all_to_all(outgoing, "pw", split_axis=0, concat_axis=0, tiled=True)
        parts.append(jnp.einsum("dckz,zcbs->dbsk", forward, sticks_back, precision=fast))
    vpsi = jnp.concatenate(parts, axis=1)
    applied = kinetic[None, None] * psi_block + vpsi
    lowered = applied.astype(jnp.bfloat16)
    gathered = lax.all_gather(lowered, "band", axis=1, tiled=True)
    intersection = intersect(gathered, psi_all, pw_count)
    return (intersection, applied)


def per_device(psi_block, psi_all, potential, stick_col):
    return per_device_rows(psi_block, psi_all, potential, stick_col)


def solution(mesh):
    return jax.shard_map(
        per_device,
        mesh=mesh,
        in_specs=(
            P(None, "band", "pw", None),
            P(None, "band", "pw", None),
            P("pw", None, None),
            P(),
        ),
        out_specs=(P(None, "pw", "band"), P(None, "band", "pw", None)),
        check_vma=False,
    )
```

profile of v0, /device:TPU:0, one launch (start us, length us, event | category | flops | bytes accessed | tf_op | source)
XLA Modules:
  0.0 94.0 jit_solution(17449898297534052666)
XLA Ops:
  0.6 1.2 %convolution_bitcast_fusion.1 = f32[128,2,1,32]{0,3,1,2:T(8,128)S(1)} fusion(f32[2,2,128,128]{3,2,1,0:T(8,128)} %constant.89.clone, f32[2,2,32,128]{3,2,1,0:T(8,128)} %param.8), kind=kOutput, calls=%fused_computation.33 | convolution fusion | flops 12582912 | bytes 327680 | tf_op jit(solution)/shard_map/dczk,cbsk->zdbs/dot_general | solution.py:117
  2.0 0.8 reshape.302
  2.7 7.3 %all-to-all-start.2 = ((f32[8,1,1024]{2,1,0:T(1,128)}), f32[8,1,1024]{2,1,0:T(1,128)S(1)}, u32[]{:S(2)}, u32[]{:S(2)}) async-start(f32[8,1,1024]{2,1,0:T(1,128)} %reshape.302), calls=%async_computation.2 | async-start | bytes 65536 | tf_op jit(solution)/shard_map/all_to_all | solution.py:118
  10.0 1.2 %convolution_bitcast_fusion.3 = f32[128,2,1,32]{0,3,1,2:T(8,128)S(1)} fusion(f32[2,2,128,128]{3,2,1,0:T(8,128)} %constant.89.clone, f32[2,2,32,128]{3,2,1,0:T(8,128)} %param.8), kind=kOutput, calls=%fused_computation.35 | convolution fusion | flops 12582912 | bytes 327680 | tf_op jit(solution)/shard_map/dczk,cbsk->zdbs/dot_general | solution.py:117
  12.6 0.8 reshape.300
  13.4 4.1 %fusion.88 = (bf16[2,64,32,128]{3,2,1,0:T(8,128)(2,1)}, bf16[2,64,32,128]{3,2,1,0:T(8,128)(2,1)}, bf16[2,64,32,128]{3,2,1,0:T(8,128)(2,1)}, bf16[2,64,32,128]{3,2,1,0:T(8,128)(2,1)S(1)}) fusion(bf16[2,256,32,128]{3,2,1,0:T(8,128)(2,1)} %param.9), kind=kLoop, calls=%fused_computation.129 | loop fusion | bytes 8388608 | tf_op jit(solution)/shard_map/slice | solution.py:85
  17.6 6.0 %all-to-all-start = ((f32[8,1,1024]{2,1,0:T(1,128)}), f32[8,1,1024]{2,1,0:T(1,128)S(1)}, u32[]{:S(2)}, u32[]{:S(2)}) async-start(f32[8,1,1024]{2,1,0:T(1,128)} %reshape.300), calls=%async_computation | async-start | bytes 65536 | tf_op jit(solution)/shard_map/all_to_all | solution.py:118
  24.1 0.7 reduce.10
  25.3 0.8 fusion
  26.1 0.8 fusion.4
  26.9 3.4 %all-to-all-done = f32[8,1,1024]{2,1,0:T(1,128)S(1)} async-done(((f32[8,1,1024]{2,1,0:T(1,128)}), f32[8,1,1024]{2,1,0:T(1,128)S(1)}, u32[]{:S(2)}, u32[]{:S(2)}) %all-to-all-start) | async-done | bytes 32800 | tf_op jit(solution)/shard_map/all_to_all | solution.py:118
  30.3 0.7 reduce.9
  31.5 1.7 %fusion.12 = f32[16,128,128]{2,1,0:T(8,128)S(1)} fusion(f32[128,256]{1,0:T(8,128)} %copy-done.9, f32[16,256]{1,0:T(8,128)S(1)} %mul.266, f32[128,256]{1,0:T(8,128)S(1)} %get-tuple-element.30, f32[16,256]{1,0:T(8,128)S(1)} %mul.257, s32[256]{0:T(256)S(1)} %get-tuple-element.28), kind=kOutput, calls=%fused_computation.16 | convolution fusion | flops 404258816 | bytes 1344512 | tf_op jit(solution)/shard_map/dot_general | solution.py:47
  33.2 1.7 %fusion.8 = f32[16,128,128]{2,1,0:T(8,128)S(1)} fusion(f32[128,256]{1,0:T(8,128)} %copy-done.9, f32[16,256]{1,0:T(8,128)S(1)} %mul.266, f32[128,256]{1,0:T(8,128)S(1)} %get-tuple-element.30, f32[16,256]{1,0:T(8,128)S(1)} %mul.257, s32[256]{0:T(256)S(1)} %get-tuple-element.28), kind=kOutput, calls=%fused_computation.12 | convolution fusion | flops 404258816 | bytes 1344512 | tf_op jit(solution)/shard_map/dot_general | solution.py:47
  44.4 0.9 fusion.66
  45.3 1.7 %add_reduce_fusion.1 = (f32[16,256]{1,0:T(8,128)S(1)}, f32[16,256]{1,0:T(8,128)S(1)}, f32[16,256]{1,0:T(8,128)S(1)}, f32[16,256]{1,0:T(8,128)S(1)}) fusion(f32[16,128,256]{2,1,0:T(8,128)S(1)} %fusion.66, f32[128,256]{1,0:T(8,128)S(1)} %copy-done.10, f32[128,256]{1,0:T(8,128)S(1)} %get-tuple-element.30, f32[16,128,256]{2,1,0:T(8,128)S(1)} %fusion.62, ...), kind=kOutput, calls=%fused_computation.11 | convolution fusion | flops 411058176 | bytes 7668736 | tf_op jit(solution)/shard_map/dot_general | solution.py:47
  47.3 0.8 reshape.306
  48.1 3.3 %all-to-all-start.1 = ((f32[8,1,1024]{2,1,0:T(1,128)}), f32[8,1,1024]{2,1,0:T(1,128)S(1)}, u32[]{:S(2)}, u32[]{:S(2)}) async-start(f32[8,1,1024]{2,1,0:T(1,128)} %reshape.306), calls=%async_computation.1 | async-start | bytes 65536 | tf_op jit(solution)/shard_map/all_to_all | solution.py:127
  51.8 0.8 reshape.304
  52.5 5.5 %all-to-all-done.1 = f32[8,1,1024]{2,1,0:T(1,128)S(1)} async-done(((f32[8,1,1024]{2,1,0:T(1,128)}), f32[8,1,1024]{2,1,0:T(1,128)S(1)}, u32[]{:S(2)}, u32[]{:S(2)}) %all-to-all-start.1) | async-done | bytes 32800 | tf_op jit(solution)/shard_map/all_to_all | solution.py:127
  58.1 4.0 %all-to-all-start.3 = ((f32[8,1,1024]{2,1,0:T(1,128)}), f32[8,1,1024]{2,1,0:T(1,128)}, u32[]{:S(2)}, u32[]{:S(2)}) async-start(f32[8,1,1024]{2,1,0:T(1,128)} %reshape.304), calls=%async_computation.3 | async-start | bytes 65536 | tf_op jit(solution)/shard_map/all_to_all | solution.py:127
  62.1 1.4 %reduce.12 = f32[8,1024]{1,0:T(8,128)} reduce(f32[8,1,1024]{2,1,0:T(1,128)S(1)} %all-to-all-done.1, f32[]{:T(128)} %broadcast.248), dimensions={1}, to_apply=%all_to_all.16.reduce_sub_computation | reduce | bytes 65540 | tf_op jit(solution)/shard_map/all_to_all | solution.py:127
  63.5 0.9 reshape.307
  65.1 3.6 %all-to-all-done.3 = f32[8,1,1024]{2,1,0:T(1,128)} async-done(((f32[8,1,1024]{2,1,0:T(1,128)}), f32[8,1,1024]{2,1,0:T(1,128)}, u32[]{:S(2)}, u32[]{:S(2)}) %all-to-all-start.3) | async-done | bytes 32800 | tf_op jit(solution)/shard_map/all_to_all | solution.py:127
  68.7 2.1 %reduce.11 = f32[8,1024]{1,0:T(8,128)} reduce(f32[8,1,1024]{2,1,0:T(1,128)} %all-to-all-done.3, f32[]{:T(128)} %broadcast.248), dimensions={1}, to_apply=%all_to_all.18.reduce_sub_computation | reduce | bytes 65540 | tf_op jit(solution)/shard_map/all_to_all | solution.py:127
  70.8 0.9 reshape.305
  72.5 1.0 %convolution_bitcast_fusion.2 = f32[2,1,32,128]{3,2,0,1:T(8,128)S(1)} fusion(f32[2,2,128,128]{3,2,1,0:T(8,128)S(1)} %copy-done.3, f32[128,2,1,32]{0,3,1,2:T(8,128)} %copy.74), kind=kOutput, calls=%fused_computation.34 | convolution fusion | flops 12582912 | bytes 327680 | tf_op jit(solution)/shard_map/dckz,zcbs->dbsk/dot_general | solution.py:128
  73.5 1.0 %convolution_bitcast_fusion = f32[2,1,32,128]{3,2,0,1:T(8,128)S(1)} fusion(f32[2,2,128,128]{3,2,1,0:T(8,128)S(1)} %copy-done.3, f32[128,2,1,32]{0,3,1,2:T(8,128)} %copy.82), kind=kOutput, calls=%fused_computation.32 | convolution fusion | flops 12582912 | bytes 327680 | tf_op jit(solution)/shard_map/dckz,zcbs->dbsk/dot_general | solution.py:128
  74.5 0.9 fusion.87
  75.4 5.4 %all_gather.3 = bf16[2,8,32,128]{3,2,0,1:T(8,128)(2,1)S(1)} all-gather(bf16[2,2,32,128]{3,2,0,1:T(8,128)(2,1)S(1)} %get-tuple-element.16), channel_id=1, replica_groups=mesh['pw'=8,'band'=4] {'band'}, dimensions={1}, use_global_device_ids=true | all-gather | bytes 163840 | tf_op jit(solution)/shard_map/all_gather | solution.py:132
  83.6 3.3 %all-to-all-start.4 = ((f32[2,8,1,256]{3,0,2,1:T(2,128)}), f32[2,8,1,256]{3,0,2,1:T(2,128)S(1)}, u32[]{:S(2)}, u32[]{:S(2)}) async-start(f32[2,8,1,256]{3,0,2,1:T(2,128)} %copy.90), calls=%async_computation.4 | async-start | bytes 32768 | tf_op jit(solution)/shard_map/all_to_all | solution.py:98
  87.5 5.9 %all-to-all-done.4 = f32[2,8,1,256]{3,0,2,1:T(2,128)S(1)} async-done(((f32[2,8,1,256]{3,0,2,1:T(2,128)}), f32[2,8,1,256]{3,0,2,1:T(2,128)S(1)}, u32[]{:S(2)}, u32[]{:S(2)}) %all-to-all-start.4) | async-done | bytes 16416 | tf_op jit(solution)/shard_map/all_to_all | solution.py:98
  (84 shorter events, 18.3 us)
Async XLA Ops:
  2.7 14.9 %all-to-all-start.2 = ((f32[8,1,1024]{2,1,0:T(1,128)}), f32[8,1,1024]{2,1,0:T(1,128)S(1)}, u32[]{:S(2)}, u32[]{:S(2)}) async-start(f32[8,1,1024]{2,1,0:T(1,128)} %reshape.302), calls=%async_computation.2 | async-start | bytes 65536 | tf_op jit(solution)/shard_map/all_to_all | solution.py:118
  12.5 13.6 %copy-start.9 = (f32[128,256]{1,0:T(8,128)}, f32[128,256]{1,0:T(8,128)S(1)}, u32[]{:S(2)}) copy-start(f32[128,256]{1,0:T(8,128)S(1)} %get-tuple-element.31) | copy-start | bytes 393220
  13.4 4.1 %copy-start.11 = (s32[256]{0:T(256)S(1)}, s32[256]{0:T(256)}, u32[]{:S(2)}) copy-start(s32[256]{0:T(256)} %param.11) | copy-start | bytes 3076
  17.6 12.7 %all-to-all-start = ((f32[8,1,1024]{2,1,0:T(1,128)}), f32[8,1,1024]{2,1,0:T(1,128)S(1)}, u32[]{:S(2)}, u32[]{:S(2)}) async-start(f32[8,1,1024]{2,1,0:T(1,128)} %reshape.300), calls=%async_computation | async-start | bytes 65536 | tf_op jit(solution)/shard_map/all_to_all | solution.py:118
  31.3 3.5 %copy-start.2 = (f32[128,128,1]{1,0,2:T(8,128)S(1)}, f32[128,128,1]{1,0,2:T(8,128)}, u32[]{:S(2)}) copy-start(f32[128,128,1]{1,0,2:T(8,128)} %constant.101) | copy-start | bytes 196612
  34.9 1.2 %copy-start = (f32[16,128,128]{2,1,0:T(8,128)S(1)}, f32[16,128,128]{2,1,0:T(8,128)}, u32[]{:S(2)}) copy-start(f32[16,128,128]{2,1,0:T(8,128)} %param.10) | copy-start | bytes 3145732
  34.9 1.2 %copy-start.7 = (f32[128,128,1]{1,0,2:T(8,128)S(1)}, f32[128,128,1]{1,0,2:T(8,128)}, u32[]{:S(2)}) copy-start(f32[128,128,1]{1,0,2:T(8,128)} %constant.103) | copy-start | bytes 196612
  36.1 0.8 copy-start.1
  39.8 0.8 copy-start.8
  44.4 0.9 copy-start.10
  47.0 25.4 %copy-start.3 = (f32[2,2,128,128]{3,2,1,0:T(8,128)S(1)}, f32[2,2,128,128]{3,2,1,0:T(8,128)}, u32[]{:S(2)}) copy-start(f32[2,2,128,128]{3,2,1,0:T(8,128)} %constant.90.clone) | copy-start | bytes 786436
  47.2 33.7 %copy-start.6 = (bf16[2,64,32,128]{3,2,1,0:T(8,128)(2,1)S(1)}, bf16[2,64,32,128]{3,2,1,0:T(8,128)(2,1)}, u32[]{:S(2)}) copy-start(bf16[2,64,32,128]{3,2,1,0:T(8,128)(2,1)} %get-tuple-element.18) | copy-start | bytes 3145732
  48.1 10.0 %all-to-all-start.1 = ((f32[8,1,1024]{2,1,0:T(1,128)}), f32[8,1,1024]{2,1,0:T(1,128)S(1)}, u32[]{:S(2)}, u32[]{:S(2)}) async-start(f32[8,1,1024]{2,1,0:T(1,128)} %reshape.306), calls=%async_computation.1 | async-start | bytes 65536 | tf_op jit(solution)/shard_map/all_to_all | solution.py:127
  58.1 10.7 %all-to-all-start.3 = ((f32[8,1,1024]{2,1,0:T(1,128)}), f32[8,1,1024]{2,1,0:T(1,128)}, u32[]{:S(2)}, u32[]{:S(2)}) async-start(f32[8,1,1024]{2,1,0:T(1,128)} %reshape.304), calls=%async_computation.3 | async-start | bytes 65536 | tf_op jit(solution)/shard_map/all_to_all | solution.py:127
  62.1 19.2 %copy-start.5 = (bf16[2,64,32,128]{3,2,1,0:T(8,128)(2,1)S(1)}, bf16[2,64,32,128]{3,2,1,0:T(8,128)(2,1)}, u32[]{:S(2)}) copy-start(bf16[2,64,32,128]{3,2,1,0:T(8,128)(2,1)} %get-tuple-element.20) | copy-start | bytes 3145732
  80.8 1.2 %copy-start.4 = (bf16[2,64,32,128]{3,2,1,0:T(8,128)(2,1)S(1)}, bf16[2,64,32,128]{3,2,1,0:T(8,128)(2,1)}, u32[]{:S(2)}) copy-start(bf16[2,64,32,128]{3,2,1,0:T(8,128)(2,1)} %get-tuple-element.19) | copy-start | bytes 3145732
  83.6 9.8 %all-to-all-start.4 = ((f32[2,8,1,256]{3,0,2,1:T(2,128)}), f32[2,8,1,256]{3,0,2,1:T(2,128)S(1)}, u32[]{:S(2)}, u32[]{:S(2)}) async-start(f32[2,8,1,256]{3,0,2,1:T(2,128)} %copy.90), calls=%async_computation.4 | async-start | bytes 32768 | tf_op jit(solution)/shard_map/all_to_all | solution.py:98
where the time goes:
time: 95.2 us; the launch traced here: 94 us
  starting transfers between devices  23.9 us (25%)
  matrix products  22 us (23%)
  waiting for transfers between devices  18.4 us (19%)
  local copies, waits for them, and re-layouts  15.8 us (17%)
  other arithmetic  7.35 us (8%)
  blocking collectives  5.43 us (6%)
  between operations  1.15 us (1%)
    dot_general x20, matrix products, mult(): jnp.dot(left, right, precision=lax.Precision.HIGH, preferred_element_type...  15.8 us
    all_to_all x2, starting transfers between devices, per_device_rows(): lax.all_to_all(z_lines, 'pw', split_axis=0, concat_axis=0, tiled=True)  13.3 us
    all_to_all x2, waiting for transfers between devices, per_device_rows(): lax.all_to_all(outgoing, 'pw', split_axis=0, concat_axis=0, tiled=True)  9.14 us
    all_to_all x2, starting transfers between devices, per_device_rows(): lax.all_to_all(outgoing, 'pw', split_axis=0, concat_axis=0, tiled=True)  7.3 us
    unnamed x33, local copies, waits for them, and re-layouts  7.24 us
    all_to_all x1, waiting for transfers between devices, intersect(): lax.all_to_all(pieces, 'pw', split_axis=1, concat_axis=1, tiled=True)  5.88 us
    all_gather x1, blocking collectives, per_device_rows(): gathered = lax.all_gather(lowered, 'band', axis=1, tiled=True)  5.43 us
    slice x1, local copies, waits for them, and re-layouts, intersect(): psi_all[:, k * width:(k + 1) * width]  4.12 us
  transfers between devices with their start and end apart: 5, of which 4 were waited for; matrix products, arithmetic and copies ran while one was open for 17% of the time, Pallas kernels for 0%

commit v1 on v0

--- a/solution.py
+++ b/solution.py
@@ -129,7 +129,15 @@
     vpsi = jnp.concatenate(parts, axis=1)
     applied = kinetic[None, None] * psi_block + vpsi
     lowered = applied.astype(jnp.bfloat16)
-    gathered = lax.all_gather(lowered, "band", axis=1, tiled=True)
+    upper = lax.axis_size("band")
+    t1, base_arr = (upper, lax.axis_index("band"))
+    gathered, z1 = (lowered, 1)
+    while z1 < t1:
+        small = lax.ppermute(gathered, "band", [(s, s ^ z1) for s in range(t1)])
+        far_arr = jnp.concatenate([gathered, small], axis=1)
+        val = jnp.concatenate([small, gathered], axis=1)
+        gathered = jnp.where(base_arr & z1 == 0, far_arr, val)
+        z1 = 2 * z1
     intersection = intersect(gathered, psi_all, pw_count)
     return (intersection, applied)
 

time: 95.2 us -> 86.6 us (0.910)
  waiting for transfers between devices: 18.4 us -> 24.2 us
  blocking collectives: 5.43 us -> 0 us
  local copies, waits for them, and re-layouts: 15.8 us -> 12.7 us
  other arithmetic: 7.35 us -> 5.17 us
  matrix products: 22 us -> 20.3 us
  starting transfers between devices: 23.9 us -> 22.4 us
    all_gather x1 -> x0, blocking collectives: 5.43 us -> none  [per_device_rows(): gathered = lax.all_gather(lowered, 'band', axis=1, tiled=True)]
    all_to_all x2, waiting for transfers between devices: 3.41 us -> 5.99 us  [per_device_rows(): lax.all_to_all(z_lines, 'pw', split_axis=0, concat_axis=0, tiled=True)]
    all_to_all x2, starting transfers between devices: 13.3 us -> 10.7 us  [per_device_rows(): lax.all_to_all(z_lines, 'pw', split_axis=0, concat_axis=0, tiled=True)]
    all_to_all x2, other arithmetic: 3.5 us -> 1.44 us  [per_device_rows(): lax.all_to_all(outgoing, 'pw', split_axis=0, concat_axis=0, tiled=True)]
    all_to_all x2, waiting for transfers between devices: 9.14 us -> 11.1 us  [per_device_rows(): lax.all_to_all(outgoing, 'pw', split_axis=0, concat_axis=0, tiled=True)]
    dot_general x20, matrix products: 15.8 us -> 14 us  [mult(): jnp.dot(left, right, precision=lax.Precision.HIGH, preferred_element_type...]
    unnamed x33 -> x23, local copies, waits for them, and re-layouts: 7.24 us -> 5.52 us
    dot_general x4, matrix products: 1.72 us -> 3.38 us  [intersect(): lax.dot_general(both, psi_all[:, k * width:(k + 1) * width], dims, prefer...]
  transfers between devices with their start and end apart: 5 -> 7, of which waited for: 4 -> 6; matrix products, arithmetic and copies ran while one was open for 17% -> 16% of each run, Pallas kernels for 0% -> 0%
where the time goes in v1:
time: 86.6 us; the launch traced here: 85.9 us
  waiting for transfers between devices  24.2 us (28%)
  starting transfers between devices  22.4 us (26%)
  matrix products  20.3 us (23%)
  local copies, waits for them, and re-layouts  12.7 us (15%)
  other arithmetic  5.17 us (6%)
  between operations  1.16 us (1%)
    dot_general x20, matrix products, mult(): jnp.dot(left, right, precision=lax.Precision.HIGH, preferred_element_type...  14 us
    all_to_all x2, waiting for transfers between devices, per_device_rows(): lax.all_to_all(outgoing, 'pw', split_axis=0, concat_axis=0, tiled=True)  11.1 us
    all_to_all x2, starting transfers between devices, per_device_rows(): lax.all_to_all(z_lines, 'pw', split_axis=0, concat_axis=0, tiled=True)  10.7 us
    all_to_all x2, starting transfers between devices, per_device_rows(): lax.all_to_all(outgoing, 'pw', split_axis=0, concat_axis=0, tiled=True)  6.67 us
    all_to_all x2, waiting for transfers between devices, per_device_rows(): lax.all_to_all(z_lines, 'pw', split_axis=0, concat_axis=0, tiled=True)  5.99 us
    all_to_all x1, waiting for transfers between devices, intersect(): lax.all_to_all(pieces, 'pw', split_axis=1, concat_axis=1, tiled=True)  5.88 us
    unnamed x23, local copies, waits for them, and re-layouts  5.52 us
    slice x1, local copies, waits for them, and re-layouts, intersect(): psi_all[:, k * width:(k + 1) * width]  4.06 us
  transfers between devices with their start and end apart: 7, of which 6 were waited for; matrix products, arithmetic and copies ran while one was open for 16% of the time, Pallas kernels for 0%

profile of v1, /device:TPU:0, one launch (start us, length us, event | category | flops | bytes accessed | tf_op | source)
XLA Modules:
  0.0 85.9 jit_solution(2463559125410159299)
XLA Ops:
  0.6 1.2 %convolution_bitcast_fusion.1 = f32[128,2,1,32]{0,3,1,2:T(8,128)S(1)} fusion(f32[2,2,128,128]{3,2,1,0:T(8,128)} %constant.95.clone, f32[2,2,32,128]{3,2,1,0:T(8,128)} %param.8), kind=kOutput, calls=%fused_computation.33 | convolution fusion | flops 12582912 | bytes 327680 | tf_op jit(solution)/shard_map/dczk,cbsk->zdbs/dot_general | solution.py:117
  2.0 0.8 reshape.302
  2.7 7.3 %all-to-all-start.2 = ((f32[8,1,1024]{2,1,0:T(1,128)}), f32[8,1,1024]{2,1,0:T(1,128)S(1)}, u32[]{:S(2)}, u32[]{:S(2)}) async-start(f32[8,1,1024]{2,1,0:T(1,128)} %reshape.302), calls=%async_computation.2 | async-start | bytes 65536 | tf_op jit(solution)/shard_map/all_to_all | solution.py:118
  10.0 1.2 %convolution_bitcast_fusion.3 = f32[128,2,1,32]{0,3,1,2:T(8,128)S(1)} fusion(f32[2,2,128,128]{3,2,1,0:T(8,128)} %constant.95.clone, f32[2,2,32,128]{3,2,1,0:T(8,128)} %param.8), kind=kOutput, calls=%fused_computation.35 | convolution fusion | flops 12582912 | bytes 327680 | tf_op jit(solution)/shard_map/dczk,cbsk->zdbs/dot_general | solution.py:117
  12.6 0.8 reshape.300
  13.4 0.8 fusion.86
  14.1 2.6 %all-to-all-done.2 = f32[8,1,1024]{2,1,0:T(1,128)S(1)} async-done(((f32[8,1,1024]{2,1,0:T(1,128)}), f32[8,1,1024]{2,1,0:T(1,128)S(1)}, u32[]{:S(2)}, u32[]{:S(2)}) %all-to-all-start.2) | async-done | bytes 32800 | tf_op jit(solution)/shard_map/all_to_all | solution.py:118
  16.7 3.4 %all-to-all-start = ((f32[8,1,1024]{2,1,0:T(1,128)}), f32[8,1,1024]{2,1,0:T(1,128)S(1)}, u32[]{:S(2)}, u32[]{:S(2)}) async-start(f32[8,1,1024]{2,1,0:T(1,128)} %reshape.300), calls=%async_computation | async-start | bytes 65536 | tf_op jit(solution)/shard_map/all_to_all | solution.py:118
  20.7 0.7 reduce.10
  21.8 0.8 fusion
  22.6 0.8 fusion.4
  23.4 3.4 %all-to-all-done = f32[8,1,1024]{2,1,0:T(1,128)S(1)} async-done(((f32[8,1,1024]{2,1,0:T(1,128)}), f32[8,1,1024]{2,1,0:T(1,128)S(1)}, u32[]{:S(2)}, u32[]{:S(2)}) %all-to-all-start) | async-done | bytes 32800 | tf_op jit(solution)/shard_map/all_to_all | solution.py:118
  26.8 0.7 reduce.9
  28.0 0.8 fusion.12
  28.8 0.8 fusion.8
  38.4 0.7 fusion.66
  39.2 0.9 %fusion.70 = f32[16,128,256]{2,1,0:T(8,128)S(1)} fusion(f32[16,128,128]{2,1,0:T(8,128)S(1)} %convolution_subtract_fusion.4, s32[256]{0:T(256)S(1)} %get-tuple-element.28), kind=kOutput, calls=%fused_computation.92 | convolution fusion | flops 402685952 | bytes 3146752 | tf_op jit(solution)/shard_map/dot_general | solution.py:47
  40.1 1.6 %add_reduce_fusion.1 = (f32[16,256]{1,0:T(8,128)S(1)}, f32[16,256]{1,0:T(8,128)S(1)}, f32[16,256]{1,0:T(8,128)S(1)}, f32[16,256]{1,0:T(8,128)S(1)}) fusion(f32[16,128,256]{2,1,0:T(8,128)S(1)} %fusion.70, f32[128,256]{1,0:T(8,128)S(1)} %get-tuple-element.31, f32[128,256]{1,0:T(8,128)S(1)} %get-tuple-element.30, f32[16,128,256]{2,1,0:T(8,128)S(1)} %fusion.66, ...), kind=kOutput, calls=%fused_computation.11 | convolution fusion | flops 411058176 | bytes 7668736 | tf_op jit(solution)/shard_map/dot_general | solution.py:47
  42.1 0.8 reshape.306
  42.8 3.3 %all-to-all-start.1 = ((f32[8,1,1024]{2,1,0:T(1,128)}), f32[8,1,1024]{2,1,0:T(1,128)S(1)}, u32[]{:S(2)}, u32[]{:S(2)}) async-start(f32[8,1,1024]{2,1,0:T(1,128)} %reshape.306), calls=%async_computation.1 | async-start | bytes 65536 | tf_op jit(solution)/shard_map/all_to_all | solution.py:127
  46.5 0.8 reshape.304
  47.3 5.5 %all-to-all-done.1 = f32[8,1,1024]{2,1,0:T(1,128)S(1)} async-done(((f32[8,1,1024]{2,1,0:T(1,128)}), f32[8,1,1024]{2,1,0:T(1,128)S(1)}, u32[]{:S(2)}, u32[]{:S(2)}) %all-to-all-start.1) | async-done | bytes 32800 | tf_op jit(solution)/shard_map/all_to_all | solution.py:127
  52.8 3.3 %all-to-all-start.3 = ((f32[8,1,1024]{2,1,0:T(1,128)}), f32[8,1,1024]{2,1,0:T(1,128)S(1)}, u32[]{:S(2)}, u32[]{:S(2)}) async-start(f32[8,1,1024]{2,1,0:T(1,128)} %reshape.304), calls=%async_computation.3 | async-start | bytes 65536 | tf_op jit(solution)/shard_map/all_to_all | solution.py:127
  56.2 0.7 reduce.12
  57.2 5.6 %all-to-all-done.3 = f32[8,1,1024]{2,1,0:T(1,128)S(1)} async-done(((f32[8,1,1024]{2,1,0:T(1,128)}), f32[8,1,1024]{2,1,0:T(1,128)S(1)}, u32[]{:S(2)}, u32[]{:S(2)}) %all-to-all-start.3) | async-done | bytes 32800 | tf_op jit(solution)/shard_map/all_to_all | solution.py:127
  62.8 0.7 reduce.11
  64.4 1.2 %collective-permute-done = bf16[2,2,32,128]{3,2,0,1:T(8,128)(2,1)S(1)} collective-permute-done((bf16[2,2,32,128]{3,2,0,1:T(8,128)(2,1)S(1)}, bf16[2,2,32,128]{3,2,0,1:T(8,128)(2,1)S(1)}, u32[]{:S(2)}, u32[]{:S(2)}) %collective-permute-start) | collective-permute-done | bytes 32800 | tf_op jit(solution)/shard_map/ppermute | solution.py:136
  65.6 1.6 %collective-permute-start.1 = (bf16[2,4,32,128]{3,2,0,1:T(8,128)(2,1)S(1)}, bf16[2,4,32,128]{3,2,0,1:T(8,128)(2,1)S(1)}, u32[]{:S(2)}, u32[]{:S(2)}) collective-permute-start(bf16[2,4,32,128]{3,2,0,1:T(8,128)(2,1)S(1)} %maximum_select_fusion.1), channel_id=1, source_target_pairs={{0,2},{1,3},{2,0},{3,1},{4,6},{5,7},{6,4},{7,5},{8,10},{9,11},{10,... | collective-permute-start | bytes 196616 | tf_op jit(solution)/shard_map/ppermute | solution.py:136
  67.2 4.1 %fusion.92 = (bf16[2,64,32,128]{3,2,1,0:T(8,128)(2,1)}, bf16[2,64,32,128]{3,2,1,0:T(8,128)(2,1)S(1)}, bf16[2,64,32,128]{3,2,1,0:T(8,128)(2,1)S(1)}, bf16[2,64,32,128]{3,2,1,0:T(8,128)(2,1)S(1)}) fusion(bf16[2,256,32,128]{3,2,1,0:T(8,128)(2,1)} %param.9), kind=kLoop, calls=%fused_computation.135 | loop fusion | bytes 8388608 | tf_op jit(solution)/shard_map/slice | solution.py:85
  71.3 1.8 %convolution_bitcast_fusion.7 = f32[16,64]{1,0:T(8,128)S(1)} fusion(bf16[2,64,32,128]{3,2,1,0:T(8,128)(2,1)} %get-tuple-element.18, bf16[2,16,32,128]{3,2,0,1:T(8,128)(2,1)S(1)} %maximum_maximum_fusion), kind=kOutput, calls=%fused_computation.39 | convolution fusion | flops 16777216 | bytes 1314816 | tf_op jit(solution)/shard_map/dot_general | solution.py:83
  75.4 3.3 %all-to-all-start.4 = ((f32[2,8,1,256]{3,0,2,1:T(2,128)}), f32[2,8,1,256]{3,0,2,1:T(2,128)S(1)}, u32[]{:S(2)}, u32[]{:S(2)}) async-start(f32[2,8,1,256]{3,0,2,1:T(2,128)} %copy.91), calls=%async_computation.4 | async-start | bytes 32768 | tf_op jit(solution)/shard_map/all_to_all | solution.py:98
  79.4 5.9 %all-to-all-done.4 = f32[2,8,1,256]{3,0,2,1:T(2,128)S(1)} async-done(((f32[2,8,1,256]{3,0,2,1:T(2,128)}), f32[2,8,1,256]{3,0,2,1:T(2,128)S(1)}, u32[]{:S(2)}, u32[]{:S(2)}) %all-to-all-start.4) | async-done | bytes 16416 | tf_op jit(solution)/shard_map/all_to_all | solution.py:98
  (79 shorter events, 16.8 us)
Async XLA Ops:
  2.7 14.0 %all-to-all-start.2 = ((f32[8,1,1024]{2,1,0:T(1,128)}), f32[8,1,1024]{2,1,0:T(1,128)S(1)}, u32[]{:S(2)}, u32[]{:S(2)}) async-start(f32[8,1,1024]{2,1,0:T(1,128)} %reshape.302), calls=%async_computation.2 | async-start | bytes 65536 | tf_op jit(solution)/shard_map/all_to_all | solution.py:118
  16.7 10.1 %all-to-all-start = ((f32[8,1,1024]{2,1,0:T(1,128)}), f32[8,1,1024]{2,1,0:T(1,128)S(1)}, u32[]{:S(2)}, u32[]{:S(2)}) async-start(f32[8,1,1024]{2,1,0:T(1,128)} %reshape.300), calls=%async_computation | async-start | bytes 65536 | tf_op jit(solution)/shard_map/all_to_all | solution.py:118
  27.9 1.7 %copy-start.2 = (f32[128,128,1]{1,0,2:T(8,128)S(1)}, f32[128,128,1]{1,0,2:T(8,128)}, u32[]{:S(2)}) copy-start(f32[128,128,1]{1,0,2:T(8,128)} %constant.107) | copy-start | bytes 196612
  29.6 1.2 %copy-start = (f32[16,128,128]{2,1,0:T(8,128)S(1)}, f32[16,128,128]{2,1,0:T(8,128)}, u32[]{:S(2)}) copy-start(f32[16,128,128]{2,1,0:T(8,128)} %param.10) | copy-start | bytes 3145732
  29.6 1.2 %copy-start.4 = (f32[128,128,1]{1,0,2:T(8,128)S(1)}, f32[128,128,1]{1,0,2:T(8,128)}, u32[]{:S(2)}) copy-start(f32[128,128,1]{1,0,2:T(8,128)} %constant.109) | copy-start | bytes 196612
  30.8 0.8 copy-start.1
  34.6 0.8 copy-start.5
  41.7 22.0 %copy-start.3 = (f32[2,2,128,128]{3,2,1,0:T(8,128)S(1)}, f32[2,2,128,128]{3,2,1,0:T(8,128)}, u32[]{:S(2)}) copy-start(f32[2,2,128,128]{3,2,1,0:T(8,128)} %constant.96.clone) | copy-start | bytes 786436
  41.7 22.6 %copy-start.6 = (f32[2,2,32,128]{3,2,1,0:T(8,128)S(1)}, f32[2,2,32,128]{3,2,1,0:T(8,128)}, u32[]{:S(2)}) copy-start(f32[2,2,32,128]{3,2,1,0:T(8,128)} %param.8) | copy-start | bytes 196612
  42.8 10.0 %all-to-all-start.1 = ((f32[8,1,1024]{2,1,0:T(1,128)}), f32[8,1,1024]{2,1,0:T(1,128)S(1)}, u32[]{:S(2)}, u32[]{:S(2)}) async-start(f32[8,1,1024]{2,1,0:T(1,128)} %reshape.306), calls=%async_computation.1 | async-start | bytes 65536 | tf_op jit(solution)/shard_map/all_to_all | solution.py:127
  52.8 10.0 %all-to-all-start.3 = ((f32[8,1,1024]{2,1,0:T(1,128)}), f32[8,1,1024]{2,1,0:T(1,128)S(1)}, u32[]{:S(2)}, u32[]{:S(2)}) async-start(f32[8,1,1024]{2,1,0:T(1,128)} %reshape.304), calls=%async_computation.3 | async-start | bytes 65536 | tf_op jit(solution)/shard_map/all_to_all | solution.py:127
  64.3 1.3 %collective-permute-start = (bf16[2,2,32,128]{3,2,0,1:T(8,128)(2,1)S(1)}, bf16[2,2,32,128]{3,2,0,1:T(8,128)(2,1)S(1)}, u32[]{:S(2)}, u32[]{:S(2)}) collective-permute-start(bf16[2,2,32,128]{3,2,0,1:T(8,128)(2,1)S(1)} %get-tuple-element.16), channel_id=1, source_target_pairs={{0,1},{1,0},{2,3},{3,2},{4,5},{5,4},{6,7},{7,6},{8,9},{9,8},{10,11... | collective-permute-start | bytes 98312 | tf_op jit(solution)/shard_map/ppermute | solution.py:136
  65.6 5.6 %collective-permute-start.1 = (bf16[2,4,32,128]{3,2,0,1:T(8,128)(2,1)S(1)}, bf16[2,4,32,128]{3,2,0,1:T(8,128)(2,1)S(1)}, u32[]{:S(2)}, u32[]{:S(2)}) collective-permute-start(bf16[2,4,32,128]{3,2,0,1:T(8,128)(2,1)S(1)} %maximum_select_fusion.1), channel_id=1, source_target_pairs={{0,2},{1,3},{2,0},{3,1},{4,6},{5,7},{6,4},{7,5},{8,10},{9,11},{10,... | collective-permute-start | bytes 196616 | tf_op jit(solution)/shard_map/ppermute | solution.py:136
  75.4 9.8 %all-to-all-start.4 = ((f32[2,8,1,256]{3,0,2,1:T(2,128)}), f32[2,8,1,256]{3,0,2,1:T(2,128)S(1)}, u32[]{:S(2)}, u32[]{:S(2)}) async-start(f32[2,8,1,256]{3,0,2,1:T(2,128)} %copy.91), calls=%async_computation.4 | async-start | bytes 32768 | tf_op jit(solution)/shard_map/all_to_all | solution.py:98
